TPU v7x, 256 devices: a whole 4x4x8 slice. The times are simulated.
256 devices in a mesh: ctx: 8 (over x, z_lo), tp: 32 (over z_hi, y, core).
Axes of the slice: x: 4, y: 4, z: 8 (z_hi: 4, z_lo: 2; z = z_hi * 2 + z_lo), core: 2. Of those that a mesh axis runs over, the one named last changes fastest.
Arguments:
- states: bfloat16 [8192, 2048], P(('ctx', 'tp')), may hold values from -6 to 6
- short_lengths: int32 [64], P('ctx'), may hold values from 1 to 64, 3072 in all
- attn_gain: float32 [2048], replicated, may hold values from 0.5 to 16
- wq: bfloat16 [2048, 2048], P(None, 'tp'), may hold values from -0.125 to 0.125
- wkv: bfloat16 [2048, 512], replicated, may hold values from -0.125 to 0.125
- wo: bfloat16 [2048, 2048], P('tp'), may hold values from -0.125 to 0.125
- mlp_gain: float32 [2048], replicated, may hold values from 0.5 to 1.5
- w_gate: bfloat16 [2048, 5632], P(None, 'tp'), may hold values from -0.125 to 0.125
- w_up: bfloat16 [2048, 5632], P(None, 'tp'), may hold values from -0.125 to 0.125
- w_down: bfloat16 [5632, 2048], P('tp'), may hold values from -0.078125 to 0.078125
Outputs:
- updated: bfloat16 [8192, 2048], P(('ctx', 'tp'))
- long_cache: bfloat16 [2, 2048, 512], P(None, 'ctx', 'tp')
- short_cache: bfloat16 [64, 64, 512], P('ctx', None, 'tp')
Inputs may be any that keep to these rules, and one draw needn't show every extreme that they name: `short_lengths`: rows of a short prompt at or beyond its length are padding; the largest length is 64.
All inputs are finite; a program needn't handle non-finite values. No bound on the sum of `short_lengths` on one device may be relied on, other than what follows from the above.
Results may differ from a plain program's by a relative error of at most 0.022.
The roundings to bfloat16 on the way count: a program that leaves them out, or rounds other values in their place, can miss the bound.
Values may be sent and summed in bfloat16 or wider, within the bound.
No kernel may reach another device: no remote copies, remote signals or barrier semaphores. Data moves between devices by JAX's collectives and lax.ppermute only.
A program may use at most 64 MiB of HBM per device.

v0:
```python
import jax
import jax.numpy as jnp
from jax import lax
from jax.sharding import PartitionSpec as P

KVH = 4
HEAD_SIZE = 64
LONG = 2
LLEN = 2048
SLEN = 64


EPS = 1e-05
THETA = 10000.0
NEG = -1e30


def rms_scale(matrix, gain):
    entries = matrix.astype(jnp.float32)
    power = jnp.mean(entries * entries, axis=-1, keepdims=True)
    return (entries * lax.rsqrt(power + EPS) * gain).astype(jnp.bfloat16)


def rotate(entries, positions):
    half_width = entries.shape[-1] // 2
    frequency = THETA ** (-jnp.arange(half_width, dtype=jnp.float32) * 2.0 / entries.shape[-1])
    angles = positions.astype(jnp.float32)[:, None] * frequency[None, :]
    cosine = jnp.cos(angles)[:, None, :]
    sine_wave = jnp.sin(angles)[:, None, :]
    first_half = entries[..., :half_width]
    second_half = entries[..., half_width:]
    return jnp.concatenate(
        [
            first_half * cosine - second_half * sine_wave,
            second_half * cosine + first_half * sine_wave,
        ],
        axis=-1,
    )


def rank_positions(ctx_rank, rank_rows, block_len, long_rows, n_blocks):
    index_row = jnp.arange(rank_rows, dtype=jnp.int32)
    half_index = index_row // block_len % 2
    offset_row = index_row % block_len
    which_block = jnp.where(half_index == 0, ctx_rank, n_blocks - 1 - ctx_rank)
    long_pos = which_block * block_len + offset_row
    short_pos = (index_row - long_rows) % SLEN
    return jnp.where(index_row < long_rows, long_pos, short_pos)


def project(matrix, positions, wq, wkv_head, heads_dev):
    row_count = matrix.shape[0]
    query_matrix = jnp.dot(matrix, wq, preferred_element_type=jnp.float32).reshape(
        row_count, heads_dev, HEAD_SIZE
    )
    query_matrix = rotate(query_matrix, positions).astype(jnp.bfloat16)
    pairs = jnp.dot(matrix, wkv_head, preferred_element_type=jnp.float32)
    key_matrix = rotate(pairs[:, None, :HEAD_SIZE], positions).astype(jnp.bfloat16)[:, 0]
    value_matrix = pairs[:, HEAD_SIZE:].astype(jnp.bfloat16)
    return jnp.concatenate(
        [query_matrix.reshape(row_count, heads_dev * HEAD_SIZE), key_matrix, value_matrix], axis=1
    )


def attend(soft_state, query_matrix, query_pos, key_matrix, value_matrix, key_pos, valid_keys):
    best_score, weight_sum, weighted = soft_state
    logit_scores = jnp.einsum(
        "rzsm,rvm->rzsv", query_matrix, key_matrix, preferred_element_type=jnp.float32
    ) * HEAD_SIZE ** (-0.5)
    allowed = (key_pos[None, :] <= query_pos[:, None])[None, None] & valid_keys[:, None, None, :]
    logit_scores = jnp.where(allowed, logit_scores, NEG)
    new_best = jnp.maximum(best_score, jnp.max(logit_scores, axis=-1))
    weights = jnp.where(allowed, jnp.exp(logit_scores - new_best[..., None]), 0.0)
    weight_sum = jnp.sum(weights, axis=-1)
    weighted = jnp.einsum(
        "awlp,ape->awle",
        weights.astype(jnp.bfloat16),
        value_matrix,
        preferred_element_type=jnp.float32,
    )
    return (new_best, weight_sum, weighted)


def per_device(states, short_lengths, attn_gain, wq, wkv, wo, mlp_gain, w_gate, w_up, w_down):
    n_ctx = lax.axis_size("ctx")
    n_tp = lax.axis_size("tp")
    ctx_rank = lax.axis_index("ctx")
    tp_index = lax.axis_index("tp")
    tok_rows = states.shape[0]
    rank_rows = tok_rows * n_tp
    n_blocks = 2 * n_ctx
    block_len = LLEN // n_blocks
    long_rows = LONG * 2 * block_len
    heads_dev = wq.shape[1] // HEAD_SIZE
    q_cols = heads_dev * HEAD_SIZE
    pair_width = 2 * HEAD_SIZE
    cache_cols = KVH * pair_width // n_tp
    kv_group = tp_index * KVH // n_tp
    wkv_head = lax.dynamic_slice_in_dim(wkv, kv_group * pair_width, pair_width, 1)
    first_col = tp_index * cache_cols - kv_group * pair_width
    positions = rank_positions(ctx_rank, rank_rows, block_len, long_rows, n_blocks)
    packed = project(
        lax.all_gather(rms_scale(states, attn_gain), "tp", axis=0, tiled=True),
        positions,
        wq,
        wkv_head,
        heads_dev,
    )
    query_matrix = packed[:, :q_cols].reshape(rank_rows, heads_dev, HEAD_SIZE)
    key_matrix = packed[:, q_cols : q_cols + HEAD_SIZE]
    value_matrix = packed[:, q_cols + HEAD_SIZE :]
    long_q = (
        query_matrix[:long_rows]
        .reshape(LONG, 2 * block_len, heads_dev, HEAD_SIZE)
        .transpose(0, 2, 1, 3)
    )
    long_k = key_matrix[:long_rows].reshape(LONG, 2, 1, block_len, HEAD_SIZE)
    long_v = value_matrix[:long_rows].reshape(LONG, 2, 1, block_len, HEAD_SIZE)
    long_qpos = positions[: 2 * block_len]
    half_pick = jnp.arange(2, dtype=jnp.int32)[:, None, None]
    long_init = (
        jnp.full((LONG, heads_dev, 2 * block_len), NEG, jnp.float32),
        jnp.zeros((LONG, heads_dev, 2 * block_len), jnp.float32),
        jnp.zeros((LONG, heads_dev, 2 * block_len, HEAD_SIZE), jnp.float32),
        jnp.zeros((LONG, 2, block_len, cache_cols), jnp.float32),
    )
    piece_k = lax.all_gather(long_k, "ctx", axis=2, tiled=True)
    piece_v = lax.all_gather(long_v, "ctx", axis=2, tiled=True)
    piece_blocks = piece_k.shape[2]
    block_ids = jnp.arange(piece_blocks, dtype=jnp.int32)
    held_blocks = jnp.stack([block_ids, n_blocks - 1 - block_ids])
    key_pos = (
        held_blocks[:, :, None] * block_len + jnp.arange(block_len, dtype=jnp.int32)
    ).reshape(-1)
    key_count = 2 * piece_blocks * block_len
    flat_k = piece_k.reshape(LONG, key_count, HEAD_SIZE)
    flat_v = piece_v.reshape(LONG, key_count, HEAD_SIZE)
    all_valid = jnp.ones((LONG, key_count), dtype=bool)
    soft_state = long_init[:3]
    soft_state = attend(soft_state, long_q, long_qpos, flat_k, flat_v, key_pos, all_valid)
    joined = jnp.concatenate([piece_k, piece_v], axis=-1)
    own_cols = lax.dynamic_slice_in_dim(joined, first_col, cache_cols, 4)
    selector = ((held_blocks[None] // 2 == ctx_rank) & (held_blocks[None] % 2 == half_pick)).astype(
        jnp.bfloat16
    )
    cache_rows = jnp.einsum(
        "ehj,phjbc->pebc", selector, own_cols, preferred_element_type=jnp.float32
    )
    folded = soft_state + (cache_rows,)
    long_out = (
        (folded[2] / folded[1][..., None])
        .astype(jnp.bfloat16)
        .transpose(0, 2, 1, 3)
        .reshape(long_rows, q_cols)
    )
    long_cache = folded[3].astype(jnp.bfloat16).reshape(LONG, 2 * block_len, cache_cols)
    short_count = short_lengths.shape[0]
    short_q = (
        query_matrix[long_rows:]
        .reshape(short_count, SLEN, heads_dev, HEAD_SIZE)
        .transpose(0, 2, 1, 3)
    )
    short_k = key_matrix[long_rows:].reshape(short_count, SLEN, HEAD_SIZE)
    short_v = value_matrix[long_rows:].reshape(short_count, SLEN, HEAD_SIZE)
    offsets = jnp.arange(SLEN, dtype=jnp.int32)
    short_valid = offsets[None, :] < short_lengths[:, None]
    short_init = (
        jnp.full((short_count, heads_dev, SLEN), NEG, jnp.float32),
        jnp.zeros((short_count, heads_dev, SLEN), jnp.float32),
        jnp.zeros((short_count, heads_dev, SLEN, HEAD_SIZE), jnp.float32),
    )
    short_state = attend(short_init, short_q, offsets, short_k, short_v, offsets, short_valid)
    short_out = (
        (short_state[2] / short_state[1][..., None])
        .astype(jnp.bfloat16)
        .transpose(0, 2, 1, 3)
        .reshape(short_count * SLEN, q_cols)
    )
    short_cache = lax.dynamic_slice_in_dim(
        jnp.concatenate([short_k, short_v], axis=-1), first_col, cache_cols, 2
    )
    attn = jnp.concatenate([long_out, short_out], axis=0)
    mixed = lax.psum_scatter(
        jnp.dot(attn, wo, preferred_element_type=jnp.float32).astype(jnp.bfloat16),
        "tp",
        scatter_dimension=0,
        tiled=True,
    ).astype(jnp.float32)
    residual = (states.astype(jnp.float32) + mixed).astype(jnp.bfloat16)
    piece = lax.all_gather(rms_scale(residual, mlp_gain), "tp", axis=0, tiled=True)
    gate = jnp.dot(piece, w_gate, preferred_element_type=jnp.float32)
    up_part = jnp.dot(piece, w_up, preferred_element_type=jnp.float32)
    hidden = (jax.nn.silu(gate) * up_part).astype(jnp.bfloat16)
    down = lax.psum_scatter(
        jnp.dot(hidden, w_down, preferred_element_type=jnp.float32).astype(jnp.bfloat16),
        "tp",
        scatter_dimension=0,
        tiled=True,
    ).astype(jnp.float32)
    updated = (residual.astype(jnp.float32) + down).astype(jnp.bfloat16)
    return (updated, long_cache, short_cache)


def solution(mesh):
    in_specs = (
        P(("ctx", "tp"), None),
        P("ctx"),
        P(),
        P(None, "tp"),
        P(),
        P("tp", None),
        P(),
        P(None, "tp"),
        P(None, "tp"),
        P("tp", None),
    )
    out_specs = (P(("ctx", "tp"), None), P(None, "ctx", "tp"), P("ctx", None, "tp"))
    return jax.shard_map(
        per_device, mesh=mesh, in_specs=in_specs, out_specs=out_specs, check_vma=False
    )
```

profile of v0, /device:TPU:2, one launch (start us, length us, event | category | flops | bytes accessed | tf_op | source)
XLA Modules:
  0.0 431.4 jit_solution(14815538953844404363)
XLA Ops:
  7.2 1.2 fusion.28
  8.4 1.7 fusion.30
  10.2 0.6 and_select_fusion.1
  10.9 1.3 iota_compare_fusion.1
  12.2 1.2 broadcast_compare_fusion
  13.4 61.1 %all-gather.3.cloned.1.call-done = bf16[1024,2048]{1,0:T(8,128)(2,1)} async-done(((bf16[32,2048]{1,0:T(8,128)(2,1)}), bf16[1024,2048]{1,0:T(8,128)(2,1)}) %all-gather.3.cloned.1.call-update) | async-done | bytes 4194320 | tf_op jit(solution)/shard_map/all_gather | solution.py:103
  74.5 3.7 fusion.105
  78.4 3.6 convolution_bitcast_fusion
  82.0 0.6 fusion.52
  83.4 0.5 fusion.8
  84.0 27.9 %all_gather.13 = bf16[2,2,8,128,64]{3,4,1,0,2:T(8,128)(2,1)S(1)} all-gather(bf16[2,2,1,128,64]{3,4,1,0,2:T(8,128)(2,1)S(1)} %copy.33), channel_id=1, replica_groups=mesh['ctx'=8,'tp'=32] {'ctx'}, dimensions={2}, use_global_device_ids=true | all-gather | bytes 589824 | tf_op jit(solution)/shard_map/all_gather | solution.py:127
  111.9 0.3 copy.34
  112.2 30.0 %all_gather.14 = bf16[2,2,8,128,64]{3,4,1,0,2:T(8,128)(2,1)S(1)} all-gather(bf16[2,2,1,128,64]{3,4,1,0,2:T(8,128)(2,1)S(1)} %copy.36), channel_id=1, replica_groups=mesh['ctx'=8,'tp'=32] {'ctx'}, dimensions={2}, use_global_device_ids=true | all-gather | bytes 589824 | tf_op jit(solution)/shard_map/all_gather | solution.py:128
  142.6 1.0 reshape.515
  143.6 1.0 reshape.513
  144.6 2.4 fusion
  147.0 1.4 fusion.1
  148.4 1.1 fusion.17
  149.6 3.2 convolution_convert_fusion.1
  152.9 99.4 %reduce-scatter.3.cloned.1.call-done = bf16[32,2048]{1,0:T(8,128)(2,1)} async-done(((bf16[1024,2048]{1,0:T(8,128)(2,1)}), bf16[32,2048]{1,0:T(8,128)(2,1)}) %reduce-scatter.3.cloned.1.call-update) | async-done | bytes 131088 | tf_op jit(solution)/shard_map/reduce_scatter | solution.py:183
  252.3 1.1 fusion.32
  253.3 1.7 fusion.34
  255.3 58.1 %all-gather.5.cloned.1.call-done = bf16[1024,2048]{1,0:T(8,128)(2,1)} async-done(((bf16[32,2048]{1,0:T(8,128)(2,1)}), bf16[1024,2048]{1,0:T(8,128)(2,1)}) %all-gather.5.cloned.1.call-update) | async-done | bytes 4194320 | tf_op jit(solution)/shard_map/all_gather | solution.py:190
  313.3 4.8 %fusion.106 = f32[1024,176]{0,1:T(8,128)} fusion(bf16[1024,2048]{1,0:T(8,128)(2,1)} %all-gather.5.cloned.1.call-done, bf16[2048,176]{0,1:T(8,128)(2,1)} %param.17), kind=kOutput, calls=%fused_computation.156 | convolution fusion | flops 738197504 | bytes 5636096 | tf_op jit(solution)/shard_map/dot_general | solution.py:191
  318.2 7.5 %convolution_convert_fusion = bf16[1024,2048]{1,0:T(8,128)(2,1)} fusion(bf16[176,2048]{1,0:T(8,128)(2,1)} %param.19, bf16[1024,2048]{1,0:T(8,128)(2,1)} %all-gather.5.cloned.1.call-done, bf16[2048,176]{0,1:T(8,128)(2,1)} %param.18, f32[1024,176]{0,1:T(8,128)} %fusion.106), kind=kOutput, calls=%fused_computation.2 | convolution fusion | flops 1479573504 | bytes 10551296 | tf_op jit(solution)/shard_map/dot_general | solution.py:195
  325.7 0.7 copy.47
  326.4 0.9 copy.46
  327.3 0.9 fusion.10
  328.2 0.6 reshape.519
  328.8 0.6 fusion.68
  329.5 93.7 %reduce-scatter.5.cloned.1.call-done = bf16[32,2048]{1,0:T(8,128)(2,1)} async-done(((bf16[1024,2048]{1,0:T(8,128)(2,1)}), bf16[32,2048]{1,0:T(8,128)(2,1)}) %reduce-scatter.5.cloned.1.call-update) | async-done | bytes 131088 | tf_op jit(solution)/shard_map/reduce_scatter | solution.py:194
  423.2 1.6 fusion.35
  (57 shorter events, 2.0 us)
Async XLA Ops:
  7.2 67.3 %copy-start = (bf16[2048,512]{1,0:T(8,128)(2,1)S(1)}, bf16[2048,512]{1,0:T(8,128)(2,1)}, u32[]{:S(2)}) copy-start(bf16[2048,512]{1,0:T(8,128)(2,1)} %param.14) | copy-start | bytes 6291460
  7.2 67.3 %all-gather.3.cloned.1.call-start = ((), (), s32[]{:S(2)}) async-start(), calls=%async_computation.2 | async-start | bytes 4325376 | tf_op jit(solution)/shard_map/all_gather | solution.py:103
  10.1 242.2 %reduce-scatter.3.cloned.1.call-start = ((), (), s32[]{:S(2)}) async-start(), calls=%async_computation.3 | async-start | bytes 4325376 | tf_op jit(solution)/shard_map/reduce_scatter | solution.py:183
  13.4 65.0 %copy-start.6 = (bf16[2048,64]{0,1:T(8,128)(2,1)S(1)}, bf16[2048,64]{0,1:T(8,128)(2,1)}, u32[]{:S(2)}) copy-start(bf16[2048,64]{0,1:T(8,128)(2,1)} %param.13) | copy-start | bytes 786436
  78.4 4.6 %copy-start.9 = (pred[8,64]{1,0:T(8,128)(4,1)S(1)}, pred[8,64]{1,0:T(8,128)(4,1)}, u32[]{:S(2)}) copy-start(pred[8,64]{1,0:T(8,128)(4,1)} %iota_compare_fusion.1) | copy-start | bytes 1540
  82.8 1.1 copy-start.5
  144.6 2.4 copy-start.1
  144.6 3.8 copy-start.4
  148.4 1.2 copy-start.7
  149.6 102.7 %copy-start.2 = (bf16[32,2048]{1,0:T(8,128)(2,1)S(1)}, bf16[32,2048]{1,0:T(8,128)(2,1)}, u32[]{:S(2)}) copy-start(bf16[32,2048]{1,0:T(8,128)(2,1)} %param.10) | copy-start | bytes 393220
  149.6 103.8 %copy-start.8 = (f32[2048]{0:T(1024)S(1)}, f32[2048]{0:T(1024)}, u32[]{:S(2)}) copy-start(f32[2048]{0:T(1024)} %param.16) | copy-start | bytes 24580
  152.8 160.5 %all-gather.5.cloned.1.call-start = ((), (), s32[]{:S(2)}) async-start(), calls=%async_computation.4 | async-start | bytes 4325376 | tf_op jit(solution)/shard_map/all_gather | solution.py:190
  255.0 168.2 %reduce-scatter.5.cloned.1.call-start = ((), (), s32[]{:S(2)}) async-start(), calls=%async_computation.5 | async-start | bytes 4325376 | tf_op jit(solution)/shard_map/reduce_scatter | solution.py:194
  325.6 97.6 %copy-start.3 = (bf16[32,2048]{1,0:T(8,128)(2,1)S(1)}, bf16[32,2048]{1,0:T(8,128)(2,1)}, u32[]{:S(2)}) copy-start(bf16[32,2048]{1,0:T(8,128)(2,1)} %reduce-scatter.3.cloned.1.call-done) | copy-start | bytes 393220
Sparse Core Ops, SparseCore 0:
  11.1 63.2 all-gather.2
  153.0 99.2 reduce-scatter.2
  255.7 57.5 all-gather.4
  325.8 97.4 reduce-scatter.4
where the time goes:
time: 432 us; the launch traced here: 431 us
  waiting for transfers between devices  312 us (72%)
  blocking collectives  57.9 us (13%)
  matrix products  28 us (6%)
  between operations  14.1 us (3%)
  other arithmetic  13.2 us (3%)
  local copies, waits for them, and re-layouts  5.59 us (1%)
    reduce_scatter x1, waiting for transfers between devices, per_device(): lax.psum_scatter(jnp.dot(attn, wo, preferred_element_type=jnp.float32).as...  99.4 us
    reduce_scatter x1, waiting for transfers between devices, per_device(): lax.psum_scatter(jnp.dot(hidden, w_down, preferred_element_type=jnp.float...  93.7 us
    all_gather x1, waiting for transfers between devices, per_device(): lax.all_gather(rms_scale(states, attn_gain), 'tp', axis=0, tiled=True)  61.1 us
    all_gather x1, waiting for transfers between devices, per_device(): lax.all_gather(rms_scale(residual, mlp_gain), 'tp', axis=0, tiled=True)  58.1 us
    all_gather x1, blocking collectives, per_device(): piece_v = lax.all_gather(long_v, 'ctx', axis=2, tiled=True)  30 us
    all_gather x1, blocking collectives, per_device(): piece_k = lax.all_gather(long_k, 'ctx', axis=2, tiled=True)  27.9 us
  transfers between devices with their start and end apart: 4, of which 4 were waited for; matrix products, arithmetic and copies ran while one was open for 2% of the time, Pallas kernels for 0%

commit v1 on v0

--- a/solution.py
+++ b/solution.py
@@ -124,8 +124,9 @@
         jnp.zeros((LONG, heads_dev, 2 * block_len, HEAD_SIZE), jnp.float32),
         jnp.zeros((LONG, 2, block_len, cache_cols), jnp.float32),
     )
-    piece_k = lax.all_gather(long_k, "ctx", axis=2, tiled=True)
-    piece_v = lax.all_gather(long_v, "ctx", axis=2, tiled=True)
+    gathered = lax.all_gather(jnp.stack([long_k[:, :, 0], long_v[:, :, 0]]), "ctx", axis=0)
+    piece_k = jnp.moveaxis(gathered[:, 0], 0, 2)
+    piece_v = jnp.moveaxis(gathered[:, 1], 0, 2)
     piece_blocks = piece_k.shape[2]
     block_ids = jnp.arange(piece_blocks, dtype=jnp.int32)
     held_blocks = jnp.stack([block_ids, n_blocks - 1 - block_ids])

time: 432 us -> 416 us (0.963)
  blocking collectives: 57.9 us -> 0 us
  waiting for transfers between devices: 312 us -> 353 us
    all_gather x2 -> x0, blocking collectives: 57.9 us -> none  [the longest x1 30 us: per_device(): piece_v = lax.all_gather(long_v, 'ctx', axis=2, tiled=True)]
    all_gather x0 -> x1, waiting for transfers between devices: none -> 36.2 us  [per_device(): lax.all_gather(jnp.stack([long_k[:, :, 0], long_v[:, :, 0]]), 'ctx', axis=0)]
  transfers between devices with their start and end apart: 4 -> 5, of which waited for: 4 -> 5; matrix products, arithmetic and copies ran while one was open for 2% -> 1% of each run, Pallas kernels for 0% -> 0%
where the time goes in v1:
time: 416 us
  waiting for transfers between devices  353 us (85%)
  matrix products  27.3 us (7%)
  between operations  14.1 us (3%)
  other arithmetic  12.1 us (3%)
  local copies, waits for them, and re-layouts  9.11 us (2%)
    reduce_scatter x1, waiting for transfers between devices, per_device(): lax.psum_scatter(jnp.dot(attn, wo, preferred_element_type=jnp.float32).as...  100 us
    reduce_scatter x1, waiting for transfers between devices, per_device(): lax.psum_scatter(jnp.dot(hidden, w_down, preferred_element_type=jnp.float...  94.4 us
    all_gather x1, waiting for transfers between devices, per_device(): lax.all_gather(rms_scale(states, attn_gain), 'tp', axis=0, tiled=True)  64.2 us
    all_gather x1, waiting for transfers between devices, per_device(): lax.all_gather(rms_scale(residual, mlp_gain), 'tp', axis=0, tiled=True)  57.9 us
    all_gather x1, waiting for transfers between devices, per_device(): lax.all_gather(jnp.stack([long_k[:, :, 0], long_v[:, :, 0]]), 'ctx', axis=0)  36.2 us
  transfers between devices with their start and end apart: 5, of which 5 were waited for; matrix products, arithmetic and copies ran while one was open for 1% of the time, Pallas kernels for 0%

profile of v1, /device:TPU:2, one launch (start us, length us, event | category | flops | bytes accessed | tf_op | source)
XLA Modules:
  0.0 415.9 jit_solution(9527063426652451580)
XLA Ops:
  7.2 1.2 fusion.28
  8.4 1.7 fusion.30
  10.3 64.2 %all-gather.5.cloned.1.call-done = bf16[1024,2048]{1,0:T(8,128)(2,1)} async-done(((bf16[32,2048]{1,0:T(8,128)(2,1)}), bf16[1024,2048]{1,0:T(8,128)(2,1)}) %all-gather.5.cloned.1.call-update) | async-done | bytes 4194320 | tf_op jit(solution)/shard_map/all_gather | solution.py:103
  74.5 3.7 fusion.106
  78.3 3.6 convolution_bitcast_fusion
  81.9 0.6 fusion.52
  82.6 0.7 pad_maximum_fusion
  83.4 0.4 copy-done.10
  83.9 1.2 broadcast_compare_fusion
  86.0 0.5 fusion.8
  86.5 36.2 %all-gather.9.cloned.1.call-done = bf16[16,2,2,128,64]{3,4,2,1,0:T(8,128)(2,1)} async-done(((bf16[2,2,2,128,64]{3,4,2,1,0:T(8,128)(2,1)}), bf16[16,2,2,128,64]{3,4,2,1,0:T(8,128)(2,1)}) %all-gather.9.cloned.1.call-update) | async-done | bytes 1048592 | tf_op jit(solution)/shard_map/all_gather | solution.py:127
  122.7 2.1 fusion.103
  124.8 0.3 copy.66
  125.2 1.0 reshape.506
  126.2 1.4 copy.65
  127.6 1.0 reshape.507
  128.6 2.4 fusion
  131.0 1.4 fusion.1
  132.4 1.1 fusion.17
  133.6 3.2 convolution_convert_fusion.1
  136.9 100.0 %reduce-scatter.3.cloned.1.call-done = bf16[32,2048]{1,0:T(8,128)(2,1)} async-done(((bf16[1024,2048]{1,0:T(8,128)(2,1)}), bf16[32,2048]{1,0:T(8,128)(2,1)}) %reduce-scatter.3.cloned.1.call-update) | async-done | bytes 131088 | tf_op jit(solution)/shard_map/reduce_scatter | solution.py:184
  236.9 1.1 fusion.32
  238.0 1.7 fusion.34
  239.9 57.9 %all-gather.7.cloned.1.call-done = bf16[1024,2048]{1,0:T(8,128)(2,1)} async-done(((bf16[32,2048]{1,0:T(8,128)(2,1)}), bf16[1024,2048]{1,0:T(8,128)(2,1)}) %all-gather.7.cloned.1.call-update) | async-done | bytes 4194320 | tf_op jit(solution)/shard_map/all_gather | solution.py:191
  297.9 4.8 %fusion.107 = f32[1024,176]{0,1:T(8,128)} fusion(bf16[1024,2048]{1,0:T(8,128)(2,1)} %all-gather.7.cloned.1.call-done, bf16[2048,176]{0,1:T(8,128)(2,1)} %param.17), kind=kOutput, calls=%fused_computation.160 | convolution fusion | flops 738197504 | bytes 5636096 | tf_op jit(solution)/shard_map/dot_general | solution.py:192
  302.7 7.5 %convolution_convert_fusion = bf16[1024,2048]{1,0:T(8,128)(2,1)} fusion(bf16[176,2048]{1,0:T(8,128)(2,1)} %param.19, bf16[1024,2048]{1,0:T(8,128)(2,1)} %all-gather.7.cloned.1.call-done, bf16[2048,176]{0,1:T(8,128)(2,1)} %param.18, f32[1024,176]{0,1:T(8,128)} %fusion.107), kind=kOutput, calls=%fused_computation.2 | convolution fusion | flops 1479573504 | bytes 10551296 | tf_op jit(solution)/shard_map/dot_general | solution.py:196
  310.2 0.6 copy-done.11
  310.9 0.9 copy.44
  311.8 0.7 fusion.68
  312.7 0.6 reshape.511
  313.3 94.4 %reduce-scatter.5.cloned.1.call-done = bf16[32,2048]{1,0:T(8,128)(2,1)} async-done(((bf16[1024,2048]{1,0:T(8,128)(2,1)}), bf16[32,2048]{1,0:T(8,128)(2,1)}) %reduce-scatter.5.cloned.1.call-update) | async-done | bytes 131088 | tf_op jit(solution)/shard_map/reduce_scatter | solution.py:195
  407.8 1.6 fusion.35
  (67 shorter events, 2.1 us)
Async XLA Ops:
  7.2 67.3 %copy-start = (bf16[2048,512]{1,0:T(8,128)(2,1)S(1)}, bf16[2048,512]{1,0:T(8,128)(2,1)}, u32[]{:S(2)}) copy-start(bf16[2048,512]{1,0:T(8,128)(2,1)} %param.14) | copy-start | bytes 6291460
  7.2 67.3 %all-gather.5.cloned.1.call-start = ((), (), s32[]{:S(2)}) async-start(), calls=%async_computation.2 | async-start | bytes 4325376 | tf_op jit(solution)/shard_map/all_gather | solution.py:103
  10.1 112.6 %all-gather.9.cloned.1.call-start = ((), (), s32[]{:S(2)}) async-start(), calls=%async_computation.6 | async-start | bytes 1179648 | tf_op jit(solution)/shard_map/all_gather | solution.py:127
  10.2 68.0 %copy-start.9 = (s32[1024]{0:T(1024)}, s32[1024]{0:T(1024)S(1)}, u32[]{:S(2)}) copy-start(s32[1024]{0:T(1024)S(1)} %fusion.78) | copy-start | bytes 12292
  10.3 68.0 %copy-start.6 = (bf16[2048,64]{0,1:T(8,128)(2,1)S(1)}, bf16[2048,64]{0,1:T(8,128)(2,1)}, u32[]{:S(2)}) copy-start(bf16[2048,64]{0,1:T(8,128)(2,1)} %param.13) | copy-start | bytes 786436
  78.2 5.1 %copy-start.12 = (s32[8]{0:T(128)S(1)}, s32[8]{0:T(128)}, u32[]{:S(2)}) copy-start(s32[8]{0:T(128)} %param.11) | copy-start | bytes 100
  78.2 5.7 %slice-start = ((s32[1024]{0:T(1024)}), s32[256]{0:T(256)S(1)}, s32[]{:S(2)}) async-start(s32[1024]{0:T(1024)} %copy-done.9), calls=%async_computation.7 | async-start | bytes 2048 | tf_op jit(solution)/shard_map/slice | solution.py:119
  83.3 153.7 %reduce-scatter.3.cloned.1.call-start = ((), (), s32[]{:S(2)}) async-start(), calls=%async_computation.3 | async-start | bytes 4325376 | tf_op jit(solution)/shard_map/reduce_scatter | solution.py:184
  83.3 0.5 copy-start.10
  85.4 39.4 %copy-start.5 = (bf16[8,64,64]{1,0,2:T(8,128)(2,1)}, bf16[8,64,64]{1,0,2:T(8,128)(2,1)S(1)}, u32[]{:S(2)}) copy-start(bf16[8,64,64]{1,0,2:T(8,128)(2,1)S(1)} %reshape.509) | copy-start | bytes 196612
  128.6 2.4 copy-start.1
  128.6 3.8 copy-start.4
  132.4 1.2 copy-start.7
  133.6 103.4 %copy-start.2 = (bf16[32,2048]{1,0:T(8,128)(2,1)S(1)}, bf16[32,2048]{1,0:T(8,128)(2,1)}, u32[]{:S(2)}) copy-start(bf16[32,2048]{1,0:T(8,128)(2,1)} %param.10) | copy-start | bytes 393220
  133.6 104.4 %copy-start.8 = (f32[2048]{0:T(1024)S(1)}, f32[2048]{0:T(1024)}, u32[]{:S(2)}) copy-start(f32[2048]{0:T(1024)} %param.16) | copy-start | bytes 24580
  136.9 161.0 %all-gather.7.cloned.1.call-start = ((), (), s32[]{:S(2)}) async-start(), calls=%async_computation.4 | async-start | bytes 4325376 | tf_op jit(solution)/shard_map/all_gather | solution.py:191
  239.7 168.1 %reduce-scatter.5.cloned.1.call-start = ((), (), s32[]{:S(2)}) async-start(), calls=%async_computation.5 | async-start | bytes 4325376 | tf_op jit(solution)/shard_map/reduce_scatter | solution.py:195
  310.2 0.7 copy-start.11
  310.2 97.6 %copy-start.3 = (bf16[32,2048]{1,0:T(8,128)(2,1)S(1)}, bf16[32,2048]{1,0:T(8,128)(2,1)}, u32[]{:S(2)}) copy-start(bf16[32,2048]{1,0:T(8,128)(2,1)} %reduce-scatter.3.cloned.1.call-done) | copy-start | bytes 393220
Sparse Core Ops, SparseCore 0:
  11.1 63.2 all-gather.4
  83.4 39.3 all-gather.8
  137.0 99.9 reduce-scatter.2
  240.2 57.5 all-gather.6
  310.3 97.3 reduce-scatter.4
